TPU v7x, 512 devices: a whole 4x4x16 slice. The times are simulated.
512 devices in a mesh: aux: 16 (over z), pair: 32 (over y, x, core).
Axes of the slice: x: 4, y: 4, z: 16, core: 2. Of those that a mesh axis runs over, the one named last changes fastest.
Arguments:
- b_tensor: bfloat16 [2560, 262144], P('aux', 'pair'), may hold values from -0.0625 to 0.0625
- eps_occ: float32 [256], replicated, may hold values from -1 to -0.3
- eps_vir: float32 [1024], replicated, may hold values from 0.05 to 3
- trial: bfloat16 [32, 262144], P(None, 'pair'), may hold values from -6 to 6
Outputs:
- trial_next: float32 [32, 262144], P(None, 'pair')
- residual: bfloat16 [32, 262144], P(None, 'pair')
- subspace: float32 [32, 32], replicated
All inputs are finite; a program needn't handle non-finite values.
Results may differ from a plain program's by a relative error of at most 0.028.
Values may be sent and summed in bfloat16 or wider, within the bound.
No kernel may reach another device: no remote copies, remote signals or barrier semaphores. Data moves between devices by JAX's collectives and lax.ppermute only.
A program may use at most 64 MiB of HBM per device.

v0:
```python
import jax
import jax.numpy as jnp
from jax import lax
from jax.sharding import PartitionSpec as P

ITERS = 2
HIGHEST_PRECISION = lax.Precision.HIGHEST


def correlation_of(first_rows, second_rows, precision=HIGHEST_PRECISION):
    return lax.dot_general(
        first_rows,
        second_rows,
        (((1,), (1,)), ((), ())),
        precision=precision,
        preferred_element_type=jnp.float32,
    )


def product(first_mat, second_mat):
    return jnp.dot(
        first_mat, second_mat, precision=HIGHEST_PRECISION, preferred_element_type=jnp.float32
    )


def pair_sum(matrices):
    return lax.all_gather(matrices, "pair").sum(0)


def aux_sum(terms):
    n_aux = lax.axis_size("aux")
    rows, cols = terms.shape
    pieces = terms.reshape(rows, n_aux, cols // n_aux)
    pieces = lax.all_to_all(pieces, "aux", 1, 1, tiled=True)
    mine = pieces.astype(jnp.float32).sum(1)
    return lax.all_gather(mine, "aux", axis=1, tiled=True)


def inverse_factor(gram_now):
    lower_tri = jnp.linalg.cholesky(gram_now)
    return lax.linalg.triangular_solve(
        lower_tri, jnp.eye(gram_now.shape[0], dtype=jnp.float32), left_side=True, lower=True
    )


def on_device(b_tensor, eps_occ, eps_vir, trial):
    block_cols = b_tensor.shape[1]
    npair_all = eps_occ.shape[0] * eps_vir.shape[0]
    k = trial.shape[0]
    everything = (eps_vir[None, :] - eps_occ[:, None]).reshape(npair_all)
    diagonal = lax.dynamic_slice_in_dim(everything, lax.axis_index("pair") * block_cols, block_cols)
    diag_row = diagonal[None, :]
    trial_now = trial
    for iteration in range(ITERS):
        if iteration == 0:
            gram_part = correlation_of(trial_now, trial_now, None)
            cross_part = correlation_of(b_tensor, trial_now, None)
        else:
            gram_part = correlation_of(trial_now, trial_now)
            cross_part = correlation_of(b_tensor.astype(jnp.float32), trial_now)
        summed = pair_sum(jnp.concatenate([gram_part / npair_all, cross_part], axis=0))
        inverse = inverse_factor(summed[:k])
        basis_now = product(inverse, trial_now.astype(jnp.float32))
        projected = lax.dot_general(
            summed[k:],
            inverse,
            (((1,), (1,)), ((), ())),
            precision=HIGHEST_PRECISION,
            preferred_element_type=jnp.float32,
        )
        projected_low = projected.astype(jnp.bfloat16)
        term = lax.dot_general(
            projected_low, b_tensor, (((0,), (0,)), ((), ())), preferred_element_type=jnp.float32
        ).astype(jnp.bfloat16)
        image_now = aux_sum(term) + diag_row * basis_now
        subspace = pair_sum(correlation_of(image_now, basis_now) / npair_all)
        residual = image_now - product(subspace, basis_now)
        trial_now = basis_now - residual / diag_row
    return (trial_now, residual.astype(jnp.bfloat16), subspace)


def solution(mesh):
    in_specs = (P("aux", "pair"), P(), P(), P(None, "pair"))
    out_specs = (P(None, "pair"), P(None, "pair"), P())
    return jax.shard_map(
        on_device, mesh=mesh, in_specs=in_specs, out_specs=out_specs, check_vma=False
    )
```

profile of v0, /device:TPU:1, one launch (start us, length us, event | category | flops | bytes accessed | tf_op | source)
XLA Modules:
  0.0 371.0 jit_solution(16617916019839826232)
XLA Ops:
  7.2 1.6 convolution_multiply_fusion.3
  9.2 2.0 fusion.19
  11.3 31.4 %all-gather.4 = f32[32,192,32]{1,2,0:T(8,128)} all-gather(f32[1,192,32]{1,2,0:T(8,128)S(1)} %maximum_bitcast_fusion), channel_id=2, replica_groups=mesh['aux'=16,'pair'=32] {'pair'}, dimensions={0}, use_global_device_ids=true | all-gather | bytes 811008 | tf_op jit(solution)/shard_map/all_gather | solution.py:27
  42.7 1.3 reduce_sum.54
  44.1 2.9 cholesky.44
  48.4 2.4 custom-call.6
  52.2 35.2 %all_to_all.10 = bf16[32,16,512]{2,0,1:T(8,128)(2,1)S(1)} all-to-all(bf16[32,16,512]{2,0,1:T(8,128)(2,1)S(1)} %bitcast.64), channel_id=1, replica_groups=mesh['aux'=16,'pair'=32] {'aux'}, dimensions={1} | all-to-all | bytes 1048576 | tf_op jit(solution)/shard_map/all_to_all | solution.py:34
  88.3 1.2 copy.28
  90.3 1.5 fusion.20
  91.8 57.8 %all-gather.9.cloned.1.call-done = f32[32,8192]{1,0:T(8,128)} async-done(((f32[32,512]{1,0:T(8,128)}), f32[32,8192]{1,0:T(8,128)}) %all-gather.9.cloned.1.call-update) | async-done | bytes 1048592 | tf_op jit(solution)/shard_map/all_gather | solution.py:36
  149.6 2.9 convolution_multiply_fusion.2
  152.6 34.8 %all-gather.1 = f32[1024,32]{1,0:T(8,128)S(1)} all-gather(f32[32,32]{1,0:T(8,128)S(1)} %copy.14), channel_id=3, replica_groups=mesh['aux'=16,'pair'=32] {'pair'}, dimensions={0}, use_global_device_ids=true | all-gather | bytes 135168 | tf_op jit(solution)/shard_map/all_gather | solution.py:27
  187.4 3.0 fusion.1
  190.5 2.4 convolution_bitcast_fusion
  194.0 26.7 %all-gather.5 = f32[32,192,32]{1,2,0:T(8,128)} all-gather(f32[1,192,32]{1,2,0:T(8,128)S(1)} %maximum_bitcast_fusion.1), channel_id=4, replica_groups=mesh['aux'=16,'pair'=32] {'pair'}, dimensions={0}, use_global_device_ids=true | all-gather | bytes 811008 | tf_op jit(solution)/shard_map/all_gather | solution.py:27
  220.7 1.3 reduce_sum.57
  222.1 2.9 cholesky.55
  226.3 2.4 custom-call.7
  230.1 30.5 %all_to_all.11 = bf16[32,16,512]{2,0,1:T(8,128)(2,1)S(1)} all-to-all(bf16[32,16,512]{2,0,1:T(8,128)(2,1)S(1)} %bitcast.66), channel_id=1, replica_groups=mesh['aux'=16,'pair'=32] {'aux'}, dimensions={1} | all-to-all | bytes 1048576 | tf_op jit(solution)/shard_map/all_to_all | solution.py:34
  261.3 3.2 fusion.21
  264.5 57.6 %all-gather.11.cloned.1.call-done = f32[32,8192]{1,0:T(8,128)} async-done(((f32[32,512]{1,0:T(8,128)}), f32[32,8192]{1,0:T(8,128)}) %all-gather.11.cloned.1.call-update) | async-done | bytes 1048592 | tf_op jit(solution)/shard_map/all_gather | solution.py:36
  322.1 2.9 convolution_multiply_fusion
  325.1 34.8 %all-gather.3 = f32[1024,32]{1,0:T(8,128)S(1)} all-gather(f32[32,32]{1,0:T(8,128)S(1)} %copy.19), channel_id=5, replica_groups=mesh['aux'=16,'pair'=32] {'pair'}, dimensions={0}, use_global_device_ids=true | all-gather | bytes 135168 | tf_op jit(solution)/shard_map/all_gather | solution.py:27
  360.0 4.2 %fusion.18 = (bf16[32,8192]{1,0:T(8,128)(2,1)}, f32[32,8192]{1,0:T(8,128)}) fusion(f32[32,8192]{1,0:T(8,128)} %fusion.21, f32[8192]{0:T(1024)S(1)} %dynamic_slice.3, f32[32,32]{1,0:T(8,128)S(1)} %reduce_sum.59, f32[32,8192]{1,0:T(8,128)} %all-gather.11.cloned.1.call-done), kind=kOutput, calls=%fused_computation.48 | convolution fusion | flops 102236160 | bytes 3706880 | tf_op jit(solution)/shard_map/dot_general | solution.py:21
  (47 shorter events, 9.6 us)
Async XLA Ops:
  7.2 2.1 copy-start
  7.2 142.5 %all-gather.9.cloned.1.call-start = ((), (), s32[]{:S(2)}) async-start(), calls=%async_computation.2 | async-start | bytes 1114112 | tf_op jit(solution)/shard_map/all_gather | solution.py:36
  51.4 36.7 %copy-start.4 = (f32[1024]{0:T(1024)S(1)}, f32[1024]{0:T(1024)}, u32[]{:S(2)}) copy-start(f32[1024]{0:T(1024)} %param.9) | copy-start | bytes 12292
  51.4 36.7 %copy-start.5 = (f32[256]{0:T(256)S(1)}, f32[256]{0:T(256)}, u32[]{:S(2)}) copy-start(f32[256]{0:T(256)} %param.8) | copy-start | bytes 3076
  52.2 38.1 %copy-start.2 = (bf16[32,8192]{1,0:T(8,128)(2,1)S(1)}, bf16[32,8192]{1,0:T(8,128)(2,1)}, u32[]{:S(2)}) copy-start(bf16[32,8192]{1,0:T(8,128)(2,1)} %param.10) | copy-start | bytes 1572868
  88.1 234.0 %all-gather.11.cloned.1.call-start = ((), (), s32[]{:S(2)}) async-start(), calls=%async_computation.3 | async-start | bytes 1114112 | tf_op jit(solution)/shard_map/all_gather | solution.py:36
  190.5 3.4 copy-start.1
  359.9 4.2 %copy-start.3 = (f32[32,32]{1,0:T(8,128)}, f32[32,32]{1,0:T(8,128)S(1)}, u32[]{:S(2)}) copy-start(f32[32,32]{1,0:T(8,128)S(1)} %reduce_sum.59) | copy-start | bytes 12292
Sparse Core Ops, SparseCore 0:
  88.2 61.3 all-gather.8
  261.4 60.6 all-gather.10
where the time goes:
time: 372 us; the launch traced here: 371 us
  blocking collectives  193 us (52%)
  waiting for transfers between devices  115 us (31%)
  matrix products  27.3 us (7%)
  other arithmetic  17.8 us (5%)
  between operations  14.3 us (4%)
    all_gather x4, blocking collectives, pair_sum(): return lax.all_gather(matrices, 'pair').sum(0)  128 us
    all_gather x2, waiting for transfers between devices, aux_sum(): return lax.all_gather(mine, 'aux', axis=1, tiled=True)  115 us
    all_to_all x2, blocking collectives, aux_sum(): pieces = lax.all_to_all(pieces, 'aux', 1, 1, tiled=True)  65.7 us
    dot_general x6, matrix products, correlation_of(): lax.dot_general(first_rows, second_rows, (((1,), (1,)), ((), ())), precis...  12.8 us
    dot_general x4, matrix products, product(): jnp.dot(first_mat, second_mat, precision=HIGHEST_PRECISION, preferred_ele...  12 us
  transfers between devices with their start and end apart: 2, of which 2 were waited for; matrix products, arithmetic and copies ran while one was open for 2% of the time, Pallas kernels for 0%

commit v1 on v0

--- a/solution.py
+++ b/solution.py
@@ -1,3 +1,4 @@
+import functools
 import jax
 import jax.numpy as jnp
 from jax import lax
@@ -5,6 +6,41 @@
 
 ITERS = 2
 HIGHEST_PRECISION = lax.Precision.HIGHEST
+
+
+def scenes_step_on(block_here, at_axis):
+    gallery = []
+    b_next, odd, local_part = (
+        jax.lax.psum(1, "aux"),
+        jax.lax.axis_index("aux"),
+        block_here.shape[at_axis],
+    )
+    for ix in [*range(b_next)]:
+        gallery.append((ix, (ix + 1) % b_next))
+    arrivals = []
+    for ix in [*range(b_next)]:
+        arrivals.append((ix, (ix - 1) % b_next))
+    aux = jnp.zeros(
+        (*block_here.shape[:at_axis], b_next * local_part, *block_here.shape[at_axis + 1 :]),
+        block_here.dtype,
+    )
+    aux = lax.dynamic_update_slice_in_dim(aux, block_here, odd * local_part, axis=at_axis)
+    parts_out = reply = block_here
+    a_now = b_next // 2
+    for hop_no in [*range(1, a_now + 1)]:
+        parts_out = jax.lax.ppermute(parts_out, axis_name="aux", perm=gallery)
+        aux = lax.dynamic_update_slice_in_dim(
+            aux, parts_out, (odd - hop_no) % b_next * local_part, axis=at_axis
+        )
+        if hop_no < b_next - a_now:
+            reply = jax.lax.ppermute(reply, "aux", arrivals)
+            aux = lax.dynamic_update_slice_in_dim(
+                aux, reply, (odd + hop_no) % b_next * local_part, axis=at_axis
+            )
+    return aux
+
+
+meet_patches_all = functools.partial(scenes_step_on, at_axis=1)
 
 
 def correlation_of(first_rows, second_rows, precision=HIGHEST_PRECISION):
@@ -33,7 +69,7 @@
     pieces = terms.reshape(rows, n_aux, cols // n_aux)
     pieces = lax.all_to_all(pieces, "aux", 1, 1, tiled=True)
     mine = pieces.astype(jnp.float32).sum(1)
-    return lax.all_gather(mine, "aux", axis=1, tiled=True)
+    return meet_patches_all(mine)
 
 
 def inverse_factor(gram_now):

time: 372 us -> 346 us (0.930)
  starting transfers between devices: 0.08 us -> 120 us
  blocking collectives: 193 us -> 126 us
  waiting for transfers between devices: 115 us -> 48.8 us
  between operations: 14.3 us -> 1.82 us
  local copies, waits for them, and re-layouts: 2.75 us -> 6.88 us
  matrix products: 27.3 us -> 23.4 us
    all_gather x2 -> x0, waiting for transfers between devices: 115 us -> none  [aux_sum(): return lax.all_gather(mine, 'aux', axis=1, tiled=True)]
    ppermute x0 -> x30, starting transfers between devices: none -> 104 us  [the longest x14 64.2 us: scenes_step_on(): reply = jax.lax.ppermute(reply, 'aux', arrivals)]
    all_to_all x2 -> x0, blocking collectives: 65.7 us -> none  [aux_sum(): pieces = lax.all_to_all(pieces, 'aux', 1, 1, tiled=True)]
    all_to_all x0 -> x2, waiting for transfers between devices: none -> 39 us  [aux_sum(): pieces = lax.all_to_all(pieces, 'aux', 1, 1, tiled=True)]
    all_to_all x0 -> x2, starting transfers between devices: none -> 16.6 us  [aux_sum(): pieces = lax.all_to_all(pieces, 'aux', 1, 1, tiled=True)]
    ppermute x0 -> x30, waiting for transfers between devices: none -> 9.77 us  [the longest x16 9.73 us: scenes_step_on(): parts_out = jax.lax.ppermute(parts_out, axis_name='aux', perm=gallery)]
  transfers between devices with their start and end apart: 2 -> 32, of which waited for: 2 -> 6; matrix products, arithmetic and copies ran while one was open for 2% -> 2% of each run, Pallas kernels for 0% -> 0%
where the time goes in v1:
time: 346 us; the launch traced here: 345 us
  blocking collectives  126 us (36%)
  starting transfers between devices  120 us (35%)
  waiting for transfers between devices  48.8 us (14%)
  matrix products  23.4 us (7%)
  other arithmetic  17.7 us (5%)
  local copies, waits for them, and re-layouts  6.88 us (2%)
    all_gather x4, blocking collectives, pair_sum(): return lax.all_gather(matrices, 'pair').sum(0)  126 us
    ppermute x14, starting transfers between devices, scenes_step_on(): reply = jax.lax.ppermute(reply, 'aux', arrivals)  64.2 us
    ppermute x16, starting transfers between devices, scenes_step_on(): parts_out = jax.lax.ppermute(parts_out, axis_name='aux', perm=gallery)  39.5 us
    all_to_all x2, waiting for transfers between devices, aux_sum(): pieces = lax.all_to_all(pieces, 'aux', 1, 1, tiled=True)  39 us
    all_to_all x2, starting transfers between devices, aux_sum(): pieces = lax.all_to_all(pieces, 'aux', 1, 1, tiled=True)  16.6 us
    dot_general x4, matrix products, product(): jnp.dot(first_mat, second_mat, precision=HIGHEST_PRECISION, preferred_ele...  11.9 us
    ppermute x16, waiting for transfers between devices, scenes_step_on(): parts_out = jax.lax.ppermute(parts_out, axis_name='aux', perm=gallery)  9.73 us
    dot_general x6, matrix products, correlation_of(): lax.dot_general(first_rows, second_rows, (((1,), (1,)), ((), ())), precis...  9.09 us
  transfers between devices with their start and end apart: 32, of which 6 were waited for; matrix products, arithmetic and copies ran while one was open for 2% of the time, Pallas kernels for 0%

profile of v1, /device:TPU:1, one launch (start us, length us, event | category | flops | bytes accessed | tf_op | source)
XLA Modules:
  0.0 344.6 jit_solution(12393088297308046360)
XLA Ops:
  4.7 31.4 %all-gather.4 = f32[32,192,32]{1,2,0:T(8,128)} all-gather(f32[1,192,32]{1,2,0:T(8,128)S(1)} %maximum_bitcast_fusion), channel_id=2, replica_groups=mesh['aux'=16,'pair'=32] {'pair'}, dimensions={0}, use_global_device_ids=true | all-gather | bytes 811008 | tf_op jit(solution)/shard_map/all_gather | solution.py:63
  46.4 12.5 %all-to-all-start = ((bf16[32,16,512]{2,0,1:T(8,128)(2,1)}), bf16[32,16,512]{2,0,1:T(8,128)(2,1)}, u32[]{:S(2)}, u32[]{:S(2)}) async-start(bf16[32,16,512]{2,0,1:T(8,128)(2,1)} %bitcast.63), calls=%async_computation | async-start | bytes 1048576 | tf_op jit(solution)/shard_map/all_to_all | solution.py:70
  62.8 19.2 %all-to-all-done = bf16[32,16,512]{2,0,1:T(8,128)(2,1)} async-done(((bf16[32,16,512]{2,0,1:T(8,128)(2,1)}), bf16[32,16,512]{2,0,1:T(8,128)(2,1)}, u32[]{:S(2)}, u32[]{:S(2)}) %all-to-all-start) | async-done | bytes 524320 | tf_op jit(solution)/shard_map/all_to_all | solution.py:70
  83.2 6.3 %collective-permute-start = (f32[32,512]{1,0:T(8,128)S(1)}, f32[32,512]{1,0:T(8,128)S(1)}, u32[]{:S(2)}, u32[]{:S(2)}) collective-permute-start(f32[32,512]{1,0:T(8,128)S(1)} %convert_reduce_fusion.1), channel_id=1, source_target_pairs={{0,32},{32,64},{64,96},{96,128},{128,160},{160,192},{192,224},{224... | collective-permute-start | bytes 196616 | tf_op jit(solution)/shard_map/ppermute | solution.py:31
  89.4 4.7 %collective-permute-start.1 = (f32[32,512]{1,0:T(8,128)S(1)}, f32[32,512]{1,0:T(8,128)S(1)}, u32[]{:S(2)}, u32[]{:S(2)}) collective-permute-start(f32[32,512]{1,0:T(8,128)S(1)} %convert_reduce_fusion.1), channel_id=1, source_target_pairs={{0,480},{32,0},{64,32},{96,64},{128,96},{160,128},{192,160},{224,1... | collective-permute-start | bytes 196616 | tf_op jit(solution)/shard_map/ppermute | solution.py:36
  96.2 4.6 %collective-permute-start.3 = (f32[32,512]{1,0:T(8,128)S(1)}, f32[32,512]{1,0:T(8,128)S(1)}, u32[]{:S(2)}, u32[]{:S(2)}) collective-permute-start(f32[32,512]{1,0:T(8,128)S(1)} %collective-permute-done.1), channel_id=1, source_target_pairs={{0,480},{32,0},{64,32},{96,64},{128,96},{160,128},{192,160},{224,1... | collective-permute-start | bytes 196616 | tf_op jit(solution)/shard_map/ppermute | solution.py:36
  102.7 4.6 %collective-permute-start.5 = (f32[32,512]{1,0:T(8,128)S(1)}, f32[32,512]{1,0:T(8,128)S(1)}, u32[]{:S(2)}, u32[]{:S(2)}) collective-permute-start(f32[32,512]{1,0:T(8,128)S(1)} %collective-permute-done.3), channel_id=1, source_target_pairs={{0,480},{32,0},{64,32},{96,64},{128,96},{160,128},{192,160},{224,1... | collective-permute-start | bytes 196616 | tf_op jit(solution)/shard_map/ppermute | solution.py:36
  109.3 4.6 %collective-permute-start.7 = (f32[32,512]{1,0:T(8,128)S(1)}, f32[32,512]{1,0:T(8,128)S(1)}, u32[]{:S(2)}, u32[]{:S(2)}) collective-permute-start(f32[32,512]{1,0:T(8,128)S(1)} %collective-permute-done.5), channel_id=1, source_target_pairs={{0,480},{32,0},{64,32},{96,64},{128,96},{160,128},{192,160},{224,1... | collective-permute-start | bytes 196616 | tf_op jit(solution)/shard_map/ppermute | solution.py:36
  115.9 4.6 %collective-permute-start.9 = (f32[32,512]{1,0:T(8,128)S(1)}, f32[32,512]{1,0:T(8,128)S(1)}, u32[]{:S(2)}, u32[]{:S(2)}) collective-permute-start(f32[32,512]{1,0:T(8,128)S(1)} %collective-permute-done.7), channel_id=1, source_target_pairs={{0,480},{32,0},{64,32},{96,64},{128,96},{160,128},{192,160},{224,1... | collective-permute-start | bytes 196616 | tf_op jit(solution)/shard_map/ppermute | solution.py:36
  123.0 4.6 %collective-permute-start.11 = (f32[32,512]{1,0:T(8,128)S(1)}, f32[32,512]{1,0:T(8,128)S(1)}, u32[]{:S(2)}, u32[]{:S(2)}) collective-permute-start(f32[32,512]{1,0:T(8,128)S(1)} %collective-permute-done.9), channel_id=1, source_target_pairs={{0,480},{32,0},{64,32},{96,64},{128,96},{160,128},{192,160},{224,1... | collective-permute-start | bytes 196616 | tf_op jit(solution)/shard_map/ppermute | solution.py:36
  129.6 4.6 %collective-permute-start.13 = (f32[32,512]{1,0:T(8,128)S(1)}, f32[32,512]{1,0:T(8,128)S(1)}, u32[]{:S(2)}, u32[]{:S(2)}) collective-permute-start(f32[32,512]{1,0:T(8,128)S(1)} %collective-permute-done.11), channel_id=1, source_target_pairs={{0,480},{32,0},{64,32},{96,64},{128,96},{160,128},{192,160},{224,1... | collective-permute-start | bytes 196616 | tf_op jit(solution)/shard_map/ppermute | solution.py:36
  136.2 4.2 %collective-permute-done.14 = f32[32,512]{1,0:T(8,128)S(1)} collective-permute-done((f32[32,512]{1,0:T(8,128)S(1)}, f32[32,512]{1,0:T(8,128)S(1)}, u32[]{:S(2)}, u32[]{:S(2)}) %collective-permute-start.14) | collective-permute-done | bytes 65568 | tf_op jit(solution)/shard_map/ppermute | solution.py:31
  142.6 34.6 %all-gather.1 = f32[1024,32]{1,0:T(8,128)S(1)} all-gather(f32[32,32]{1,0:T(8,128)S(1)} %copy.14), channel_id=3, replica_groups=mesh['aux'=16,'pair'=32] {'pair'}, dimensions={0}, use_global_device_ids=true | all-gather | bytes 135168 | tf_op jit(solution)/shard_map/all_gather | solution.py:63
  183.8 25.0 %all-gather.5 = f32[32,192,32]{1,2,0:T(8,128)} all-gather(f32[1,192,32]{1,2,0:T(8,128)S(1)} %maximum_bitcast_fusion.1), channel_id=4, replica_groups=mesh['aux'=16,'pair'=32] {'pair'}, dimensions={0}, use_global_device_ids=true | all-gather | bytes 811008 | tf_op jit(solution)/shard_map/all_gather | solution.py:63
  226.3 19.8 %all-to-all-done.1 = bf16[32,16,512]{2,0,1:T(8,128)(2,1)S(1)} async-done(((bf16[32,16,512]{2,0,1:T(8,128)(2,1)}), bf16[32,16,512]{2,0,1:T(8,128)(2,1)S(1)}, u32[]{:S(2)}, u32[]{:S(2)}) %all-to-all-start.1) | async-done | bytes 524320 | tf_op jit(solution)/shard_map/all_to_all | solution.py:70
  246.2 6.4 %collective-permute-start.15 = (f32[32,512]{1,0:T(8,128)S(1)}, f32[32,512]{1,0:T(8,128)S(1)}, u32[]{:S(2)}, u32[]{:S(2)}) collective-permute-start(f32[32,512]{1,0:T(8,128)S(1)} %convert_reduce_fusion), channel_id=1, source_target_pairs={{0,32},{32,64},{64,96},{96,128},{128,160},{160,192},{192,224},{224... | collective-permute-start | bytes 196616 | tf_op jit(solution)/shard_map/ppermute | solution.py:31
  252.6 4.7 %collective-permute-start.16 = (f32[32,512]{1,0:T(8,128)S(1)}, f32[32,512]{1,0:T(8,128)S(1)}, u32[]{:S(2)}, u32[]{:S(2)}) collective-permute-start(f32[32,512]{1,0:T(8,128)S(1)} %convert_reduce_fusion), channel_id=1, source_target_pairs={{0,480},{32,0},{64,32},{96,64},{128,96},{160,128},{192,160},{224,1... | collective-permute-start | bytes 196616 | tf_op jit(solution)/shard_map/ppermute | solution.py:36
  259.4 4.6 %collective-permute-start.18 = (f32[32,512]{1,0:T(8,128)S(1)}, f32[32,512]{1,0:T(8,128)S(1)}, u32[]{:S(2)}, u32[]{:S(2)}) collective-permute-start(f32[32,512]{1,0:T(8,128)S(1)} %collective-permute-done.16), channel_id=1, source_target_pairs={{0,480},{32,0},{64,32},{96,64},{128,96},{160,128},{192,160},{224,1... | collective-permute-start | bytes 196616 | tf_op jit(solution)/shard_map/ppermute | solution.py:36
  265.9 4.6 %collective-permute-start.20 = (f32[32,512]{1,0:T(8,128)S(1)}, f32[32,512]{1,0:T(8,128)S(1)}, u32[]{:S(2)}, u32[]{:S(2)}) collective-permute-start(f32[32,512]{1,0:T(8,128)S(1)} %collective-permute-done.18), channel_id=1, source_target_pairs={{0,480},{32,0},{64,32},{96,64},{128,96},{160,128},{192,160},{224,1... | collective-permute-start | bytes 196616 | tf_op jit(solution)/shard_map/ppermute | solution.py:36
  272.5 4.6 %collective-permute-start.22 = (f32[32,512]{1,0:T(8,128)S(1)}, f32[32,512]{1,0:T(8,128)S(1)}, u32[]{:S(2)}, u32[]{:S(2)}) collective-permute-start(f32[32,512]{1,0:T(8,128)S(1)} %collective-permute-done.20), channel_id=1, source_target_pairs={{0,480},{32,0},{64,32},{96,64},{128,96},{160,128},{192,160},{224,1... | collective-permute-start | bytes 196616 | tf_op jit(solution)/shard_map/ppermute | solution.py:36
  279.1 4.6 %collective-permute-start.24 = (f32[32,512]{1,0:T(8,128)S(1)}, f32[32,512]{1,0:T(8,128)S(1)}, u32[]{:S(2)}, u32[]{:S(2)}) collective-permute-start(f32[32,512]{1,0:T(8,128)S(1)} %collective-permute-done.22), channel_id=1, source_target_pairs={{0,480},{32,0},{64,32},{96,64},{128,96},{160,128},{192,160},{224,1... | collective-permute-start | bytes 196616 | tf_op jit(solution)/shard_map/ppermute | solution.py:36
  286.2 4.6 %collective-permute-start.26 = (f32[32,512]{1,0:T(8,128)S(1)}, f32[32,512]{1,0:T(8,128)S(1)}, u32[]{:S(2)}, u32[]{:S(2)}) collective-permute-start(f32[32,512]{1,0:T(8,128)S(1)} %collective-permute-done.24), channel_id=1, source_target_pairs={{0,480},{32,0},{64,32},{96,64},{128,96},{160,128},{192,160},{224,1... | collective-permute-start | bytes 196616 | tf_op jit(solution)/shard_map/ppermute | solution.py:36
  292.8 4.6 %collective-permute-start.28 = (f32[32,512]{1,0:T(8,128)S(1)}, f32[32,512]{1,0:T(8,128)S(1)}, u32[]{:S(2)}, u32[]{:S(2)}) collective-permute-start(f32[32,512]{1,0:T(8,128)S(1)} %collective-permute-done.26), channel_id=1, source_target_pairs={{0,480},{32,0},{64,32},{96,64},{128,96},{160,128},{192,160},{224,1... | collective-permute-start | bytes 196616 | tf_op jit(solution)/shard_map/ppermute | solution.py:36
  305.8 34.7 %all-gather.3 = f32[1024,32]{1,0:T(8,128)S(1)} all-gather(f32[32,32]{1,0:T(8,128)S(1)} %copy.19), channel_id=5, replica_groups=mesh['aux'=16,'pair'=32] {'pair'}, dimensions={0}, use_global_device_ids=true | all-gather | bytes 135168 | tf_op jit(solution)/shard_map/all_gather | solution.py:63
  (145 shorter events, 84.5 us)
Async XLA Ops:
  46.4 35.5 %all-to-all-start = ((bf16[32,16,512]{2,0,1:T(8,128)(2,1)}), bf16[32,16,512]{2,0,1:T(8,128)(2,1)}, u32[]{:S(2)}, u32[]{:S(2)}) async-start(bf16[32,16,512]{2,0,1:T(8,128)(2,1)} %bitcast.63), calls=%async_computation | async-start | bytes 1048576 | tf_op jit(solution)/shard_map/all_to_all | solution.py:70
  83.2 11.1 %collective-permute-start = (f32[32,512]{1,0:T(8,128)S(1)}, f32[32,512]{1,0:T(8,128)S(1)}, u32[]{:S(2)}, u32[]{:S(2)}) collective-permute-start(f32[32,512]{1,0:T(8,128)S(1)} %convert_reduce_fusion.1), channel_id=1, source_target_pairs={{0,32},{32,64},{64,96},{96,128},{128,160},{160,192},{192,224},{224... | collective-permute-start | bytes 196616 | tf_op jit(solution)/shard_map/ppermute | solution.py:31
  89.4 6.7 %collective-permute-start.1 = (f32[32,512]{1,0:T(8,128)S(1)}, f32[32,512]{1,0:T(8,128)S(1)}, u32[]{:S(2)}, u32[]{:S(2)}) collective-permute-start(f32[32,512]{1,0:T(8,128)S(1)} %convert_reduce_fusion.1), channel_id=1, source_target_pairs={{0,480},{32,0},{64,32},{96,64},{128,96},{160,128},{192,160},{224,1... | collective-permute-start | bytes 196616 | tf_op jit(solution)/shard_map/ppermute | solution.py:36
  94.2 6.6 %collective-permute-start.2 = (f32[32,512]{1,0:T(8,128)S(1)}, f32[32,512]{1,0:T(8,128)S(1)}, u32[]{:S(2)}, u32[]{:S(2)}) collective-permute-start(f32[32,512]{1,0:T(8,128)S(1)} %collective-permute-done), channel_id=1, source_target_pairs={{0,32},{32,64},{64,96},{96,128},{128,160},{160,192},{192,224},{224... | collective-permute-start | bytes 196616 | tf_op jit(solution)/shard_map/ppermute | solution.py:31
  96.2 6.6 %collective-permute-start.3 = (f32[32,512]{1,0:T(8,128)S(1)}, f32[32,512]{1,0:T(8,128)S(1)}, u32[]{:S(2)}, u32[]{:S(2)}) collective-permute-start(f32[32,512]{1,0:T(8,128)S(1)} %collective-permute-done.1), channel_id=1, source_target_pairs={{0,480},{32,0},{64,32},{96,64},{128,96},{160,128},{192,160},{224,1... | collective-permute-start | bytes 196616 | tf_op jit(solution)/shard_map/ppermute | solution.py:36
  100.8 6.6 %collective-permute-start.4 = (f32[32,512]{1,0:T(8,128)S(1)}, f32[32,512]{1,0:T(8,128)S(1)}, u32[]{:S(2)}, u32[]{:S(2)}) collective-permute-start(f32[32,512]{1,0:T(8,128)S(1)} %collective-permute-done.2), channel_id=1, source_target_pairs={{0,32},{32,64},{64,96},{96,128},{128,160},{160,192},{192,224},{224... | collective-permute-start | bytes 196616 | tf_op jit(solution)/shard_map/ppermute | solution.py:31
  102.7 6.6 %collective-permute-start.5 = (f32[32,512]{1,0:T(8,128)S(1)}, f32[32,512]{1,0:T(8,128)S(1)}, u32[]{:S(2)}, u32[]{:S(2)}) collective-permute-start(f32[32,512]{1,0:T(8,128)S(1)} %collective-permute-done.3), channel_id=1, source_target_pairs={{0,480},{32,0},{64,32},{96,64},{128,96},{160,128},{192,160},{224,1... | collective-permute-start | bytes 196616 | tf_op jit(solution)/shard_map/ppermute | solution.py:36
  107.4 6.6 %collective-permute-start.6 = (f32[32,512]{1,0:T(8,128)S(1)}, f32[32,512]{1,0:T(8,128)S(1)}, u32[]{:S(2)}, u32[]{:S(2)}) collective-permute-start(f32[32,512]{1,0:T(8,128)S(1)} %collective-permute-done.4), channel_id=1, source_target_pairs={{0,32},{32,64},{64,96},{96,128},{128,160},{160,192},{192,224},{224... | collective-permute-start | bytes 196616 | tf_op jit(solution)/shard_map/ppermute | solution.py:31
  109.3 6.6 %collective-permute-start.7 = (f32[32,512]{1,0:T(8,128)S(1)}, f32[32,512]{1,0:T(8,128)S(1)}, u32[]{:S(2)}, u32[]{:S(2)}) collective-permute-start(f32[32,512]{1,0:T(8,128)S(1)} %collective-permute-done.5), channel_id=1, source_target_pairs={{0,480},{32,0},{64,32},{96,64},{128,96},{160,128},{192,160},{224,1... | collective-permute-start | bytes 196616 | tf_op jit(solution)/shard_map/ppermute | solution.py:36
  113.9 7.2 %collective-permute-start.8 = (f32[32,512]{1,0:T(8,128)S(1)}, f32[32,512]{1,0:T(8,128)S(1)}, u32[]{:S(2)}, u32[]{:S(2)}) collective-permute-start(f32[32,512]{1,0:T(8,128)S(1)} %collective-permute-done.6), channel_id=1, source_target_pairs={{0,32},{32,64},{64,96},{96,128},{128,160},{160,192},{192,224},{224... | collective-permute-start | bytes 196616 | tf_op jit(solution)/shard_map/ppermute | solution.py:31
  115.9 7.1 %collective-permute-start.9 = (f32[32,512]{1,0:T(8,128)S(1)}, f32[32,512]{1,0:T(8,128)S(1)}, u32[]{:S(2)}, u32[]{:S(2)}) collective-permute-start(f32[32,512]{1,0:T(8,128)S(1)} %collective-permute-done.7), channel_id=1, source_target_pairs={{0,480},{32,0},{64,32},{96,64},{128,96},{160,128},{192,160},{224,1... | collective-permute-start | bytes 196616 | tf_op jit(solution)/shard_map/ppermute | solution.py:36
  123.0 6.6 %collective-permute-start.11 = (f32[32,512]{1,0:T(8,128)S(1)}, f32[32,512]{1,0:T(8,128)S(1)}, u32[]{:S(2)}, u32[]{:S(2)}) collective-permute-start(f32[32,512]{1,0:T(8,128)S(1)} %collective-permute-done.9), channel_id=1, source_target_pairs={{0,480},{32,0},{64,32},{96,64},{128,96},{160,128},{192,160},{224,1... | collective-permute-start | bytes 196616 | tf_op jit(solution)/shard_map/ppermute | solution.py:36
  127.7 6.6 %collective-permute-start.12 = (f32[32,512]{1,0:T(8,128)S(1)}, f32[32,512]{1,0:T(8,128)S(1)}, u32[]{:S(2)}, u32[]{:S(2)}) collective-permute-start(f32[32,512]{1,0:T(8,128)S(1)} %collective-permute-done.10), channel_id=1, source_target_pairs={{0,32},{32,64},{64,96},{96,128},{128,160},{160,192},{192,224},{224... | collective-permute-start | bytes 196616 | tf_op jit(solution)/shard_map/ppermute | solution.py:31
  129.6 6.6 %collective-permute-start.13 = (f32[32,512]{1,0:T(8,128)S(1)}, f32[32,512]{1,0:T(8,128)S(1)}, u32[]{:S(2)}, u32[]{:S(2)}) collective-permute-start(f32[32,512]{1,0:T(8,128)S(1)} %collective-permute-done.11), channel_id=1, source_target_pairs={{0,480},{32,0},{64,32},{96,64},{128,96},{160,128},{192,160},{224,1... | collective-permute-start | bytes 196616 | tf_op jit(solution)/shard_map/ppermute | solution.py:36
  219.0 27.2 %all-to-all-start.1 = ((bf16[32,16,512]{2,0,1:T(8,128)(2,1)}), bf16[32,16,512]{2,0,1:T(8,128)(2,1)S(1)}, u32[]{:S(2)}, u32[]{:S(2)}) async-start(bf16[32,16,512]{2,0,1:T(8,128)(2,1)} %bitcast.64), calls=%async_computation.1 | async-start | bytes 1048576 | tf_op jit(solution)/shard_map/all_to_all | solution.py:70
  246.2 11.2 %collective-permute-start.15 = (f32[32,512]{1,0:T(8,128)S(1)}, f32[32,512]{1,0:T(8,128)S(1)}, u32[]{:S(2)}, u32[]{:S(2)}) collective-permute-start(f32[32,512]{1,0:T(8,128)S(1)} %convert_reduce_fusion), channel_id=1, source_target_pairs={{0,32},{32,64},{64,96},{96,128},{128,160},{160,192},{192,224},{224... | collective-permute-start | bytes 196616 | tf_op jit(solution)/shard_map/ppermute | solution.py:31
  252.6 6.8 %collective-permute-start.16 = (f32[32,512]{1,0:T(8,128)S(1)}, f32[32,512]{1,0:T(8,128)S(1)}, u32[]{:S(2)}, u32[]{:S(2)}) collective-permute-start(f32[32,512]{1,0:T(8,128)S(1)} %convert_reduce_fusion), channel_id=1, source_target_pairs={{0,480},{32,0},{64,32},{96,64},{128,96},{160,128},{192,160},{224,1... | collective-permute-start | bytes 196616 | tf_op jit(solution)/shard_map/ppermute | solution.py:36
  257.4 6.6 %collective-permute-start.17 = (f32[32,512]{1,0:T(8,128)S(1)}, f32[32,512]{1,0:T(8,128)S(1)}, u32[]{:S(2)}, u32[]{:S(2)}) collective-permute-start(f32[32,512]{1,0:T(8,128)S(1)} %collective-permute-done.15), channel_id=1, source_target_pairs={{0,32},{32,64},{64,96},{96,128},{128,160},{160,192},{192,224},{224... | collective-permute-start | bytes 196616 | tf_op jit(solution)/shard_map/ppermute | solution.py:31
  259.4 6.6 %collective-permute-start.18 = (f32[32,512]{1,0:T(8,128)S(1)}, f32[32,512]{1,0:T(8,128)S(1)}, u32[]{:S(2)}, u32[]{:S(2)}) collective-permute-start(f32[32,512]{1,0:T(8,128)S(1)} %collective-permute-done.16), channel_id=1, source_target_pairs={{0,480},{32,0},{64,32},{96,64},{128,96},{160,128},{192,160},{224,1... | collective-permute-start | bytes 196616 | tf_op jit(solution)/shard_map/ppermute | solution.py:36
  264.0 6.6 %collective-permute-start.19 = (f32[32,512]{1,0:T(8,128)S(1)}, f32[32,512]{1,0:T(8,128)S(1)}, u32[]{:S(2)}, u32[]{:S(2)}) collective-permute-start(f32[32,512]{1,0:T(8,128)S(1)} %collective-permute-done.17), channel_id=1, source_target_pairs={{0,32},{32,64},{64,96},{96,128},{128,160},{160,192},{192,224},{224... | collective-permute-start | bytes 196616 | tf_op jit(solution)/shard_map/ppermute | solution.py:31
  277.1 7.2 %collective-permute-start.23 = (f32[32,512]{1,0:T(8,128)S(1)}, f32[32,512]{1,0:T(8,128)S(1)}, u32[]{:S(2)}, u32[]{:S(2)}) collective-permute-start(f32[32,512]{1,0:T(8,128)S(1)} %collective-permute-done.21), channel_id=1, source_target_pairs={{0,32},{32,64},{64,96},{96,128},{128,160},{160,192},{192,224},{224... | collective-permute-start | bytes 196616 | tf_op jit(solution)/shard_map/ppermute | solution.py:31
  279.1 7.1 %collective-permute-start.24 = (f32[32,512]{1,0:T(8,128)S(1)}, f32[32,512]{1,0:T(8,128)S(1)}, u32[]{:S(2)}, u32[]{:S(2)}) collective-permute-start(f32[32,512]{1,0:T(8,128)S(1)} %collective-permute-done.22), channel_id=1, source_target_pairs={{0,480},{32,0},{64,32},{96,64},{128,96},{160,128},{192,160},{224,1... | collective-permute-start | bytes 196616 | tf_op jit(solution)/shard_map/ppermute | solution.py:36
  286.2 6.6 %collective-permute-start.26 = (f32[32,512]{1,0:T(8,128)S(1)}, f32[32,512]{1,0:T(8,128)S(1)}, u32[]{:S(2)}, u32[]{:S(2)}) collective-permute-start(f32[32,512]{1,0:T(8,128)S(1)} %collective-permute-done.24), channel_id=1, source_target_pairs={{0,480},{32,0},{64,32},{96,64},{128,96},{160,128},{192,160},{224,1... | collective-permute-start | bytes 196616 | tf_op jit(solution)/shard_map/ppermute | solution.py:36
  292.8 6.6 %collective-permute-start.28 = (f32[32,512]{1,0:T(8,128)S(1)}, f32[32,512]{1,0:T(8,128)S(1)}, u32[]{:S(2)}, u32[]{:S(2)}) collective-permute-start(f32[32,512]{1,0:T(8,128)S(1)} %collective-permute-done.26), channel_id=1, source_target_pairs={{0,480},{32,0},{64,32},{96,64},{128,96},{160,128},{192,160},{224,1... | collective-permute-start | bytes 196616 | tf_op jit(solution)/shard_map/ppermute | solution.py:36
  (18 other events, 224.7 us)
